TPU v7x, 512 devices: a whole 4x4x16 slice. The times are simulated.
512 devices in a mesh: fsdp: 32 (over x_lo, z), tp: 16 (over x_hi, y, core).
Axes of the slice: x: 4 (x_hi: 2, x_lo: 2; x = x_hi * 2 + x_lo), y: 4, z: 16, core: 2. Of those that a mesh axis runs over, the one named last changes fastest.
Arguments:
- activations: bfloat16 [16384, 4096], P(('fsdp', 'tp')), may hold values from -6 to 6
- norm_gain: float32 [4096], replicated, may hold values from 0.5 to 1.5
- proj_weight: bfloat16 [3, 4096, 4096], P(None, 'fsdp', 'tp'), may hold values from -0.09375 to 0.09375
- short_filter: float32 [256, 7], P('tp'), may hold values from -3 to 3
- segment_ids: int32 [32, 512], P('fsdp'), may hold values from 0 to 7, never falling along the last dimension, each value on 1 to 256 neighbouring positions
- needle_pos: int32 [32, 16], P('fsdp'), may hold values from 0 to 511
- readout: float32 [4096], replicated, may hold values from -6 to 6
Outputs:
- mixer_out: bfloat16 [16384, 4096], P(('fsdp', 'tp'))
- needle_score: float32 [32, 16], P('fsdp')
Inputs may be any that keep to these rules, and one draw needn't show every extreme that they name: segment_ids never fall along a slab; each document covers 1 to 256 positions.
All inputs are finite; a program needn't handle non-finite values.
Results may differ from a plain program's by a relative error of at most 0.0068.
Values may be sent and summed in bfloat16 or wider, within the bound.
No kernel may reach another device: no remote copies, remote signals or barrier semaphores. Data moves between devices by JAX's collectives and lax.ppermute only.
A program may use at most 64 MiB of HBM per device.

v0:
```python
import math
import jax
import jax.numpy as jnp
from jax import lax
from jax.sharding import PartitionSpec as P

EPSILON = 1e-06


def short_conv(gated_prod, tap_table, segments):
    length = gated_prod.shape[0]
    filtered = jnp.zeros(gated_prod.shape, jnp.float32)
    for offset in range(tap_table.shape[1]):
        shifted = jnp.pad(gated_prod, ((offset, 0), (0, 0)))[:length]
        earlier = jnp.pad(segments, (offset, 0), constant_values=-1)[:length]
        same_doc = (earlier == segments).astype(jnp.float32)
        filtered = filtered + shifted * same_doc[:, None] * tap_table[:, offset][None, :]
    return filtered


def local(activations, norm_gain, proj_weight, short_filter, segment_ids, needle_pos, readout):
    model_width = activations.shape[1]
    local_rows = activations.shape[0]
    values = activations.astype(jnp.float32)
    scaled = lax.rsqrt(jnp.mean(values * values, axis=1, keepdims=True) + EPSILON)
    normed = (values * scaled * norm_gain[None, :]).astype(jnp.bfloat16)
    slab_rows = lax.all_gather(normed, "tp", axis=0, tiled=True)
    channels = proj_weight.shape[2]
    projected = jnp.einsum(
        "sk,ikc->isc",
        slab_rows,
        lax.all_gather(proj_weight, "fsdp", axis=1, tiled=True),
        preferred_element_type=jnp.float32,
    )
    gated_prod = projected[1] * projected[2]
    tap_table = jnp.repeat(short_filter, channels // short_filter.shape[0], axis=0)
    filtered = short_conv(gated_prod, tap_table, segment_ids[0])
    mixed_local = (projected[0] * filtered).astype(jnp.bfloat16)
    device_rank = lax.axis_index("tp")
    full_rows = lax.all_gather(mixed_local, "tp", axis=1, tiled=True)
    own_rows = lax.dynamic_slice_in_dim(full_rows, device_rank * local_rows, local_rows, 0)
    positions = needle_pos[0]
    local_pos = positions - device_rank * local_rows
    picker = (local_pos[:, None] == jnp.arange(local_rows, dtype=jnp.int32)[None, :]).astype(
        jnp.bfloat16
    )
    picked = jnp.dot(picker, own_rows, preferred_element_type=jnp.float32)
    partial_sum = jnp.sum(picked * readout[None, :], axis=1)
    summed_score = lax.psum(partial_sum, "tp")
    needle_score = (summed_score / math.sqrt(model_width))[None, :]
    return (own_rows, needle_score)


def solution(mesh):
    in_specs = (
        P(("fsdp", "tp"), None),
        P(),
        P(None, "fsdp", "tp"),
        P("tp", None),
        P("fsdp", None),
        P("fsdp", None),
        P(),
    )
    out_specs = (P(("fsdp", "tp"), None), P("fsdp", None))
    return jax.shard_map(local, mesh=mesh, in_specs=in_specs, out_specs=out_specs, check_vma=False)
```

profile of v0, /device:TPU:1, one launch (start us, length us, event | category | flops | bytes accessed | tf_op | source)
XLA Modules:
  0.0 348.2 jit_solution(14428492473865925798)
XLA Ops:
  7.2 0.0 all-gather.4.cloned.1.call-start
  7.2 1.1 fusion.26
  8.3 1.8 fusion.28
  10.1 0.0 all-gather.4.cloned.1.call-update
  10.1 0.0 all-gather.6.cloned.1.call-start
  10.2 0.7 all-gather.6.cloned.1.call-update
  10.9 0.0 all-gather.8.cloned.1.call-start
  10.9 0.8 broadcast_in_dim.4
  11.7 0.1 reshape.38
  11.8 1.0 fusion.42
  12.8 0.0 copy-start.2
  12.8 0.0 copy-start.1
  12.9 75.4 %all-gather.4.cloned.1.call-done = bf16[512,4096]{1,0:T(8,128)(2,1)} async-done(((bf16[32,4096]{1,0:T(8,128)(2,1)}), bf16[512,4096]{1,0:T(8,128)(2,1)}) %all-gather.4.cloned.1.call-update) | async-done | bytes 4194320 | tf_op jit(solution)/shard_map/all_gather | solution.py:27
  88.3 123.8 %all-gather.6.cloned.1.call-done = bf16[3,4096,256]{2,1,0:T(8,128)(2,1)} async-done(((bf16[3,128,256]{2,1,0:T(8,128)(2,1)}), bf16[3,4096,256]{2,1,0:T(8,128)(2,1)}) %all-gather.6.cloned.1.call-update) | async-done | bytes 6291472 | tf_op jit(solution)/shard_map/all_gather | solution.py:32
  212.0 7.0 %fusion.2 = f32[3,512,256]{2,1,0:T(8,128)S(1)} fusion(bf16[3,4096,256]{2,1,0:T(8,128)(2,1)} %all-gather.6.cloned.1.call-done, bf16[512,4096]{1,0:T(8,128)(2,1)} %all-gather.4.cloned.1.call-done), kind=kOutput, calls=%fused_computation.3 | convolution fusion | flops 3221225472 | bytes 12058624 | tf_op jit(solution)/shard_map/sk,ikc->isc/dot_general | solution.py:29
  219.1 0.1 fusion.29
  219.1 1.5 fusion.15
  220.6 0.0 all-gather.8.cloned.1.call-update
  220.6 0.0 copy-done.2
  220.7 86.4 %all-gather.8.cloned.1.call-done = bf16[512,4096]{1,0:T(8,128)(2,1)} async-done(((bf16[512,256]{1,0:T(8,128)(2,1)}), bf16[512,4096]{1,0:T(8,128)(2,1)}) %all-gather.8.cloned.1.call-update) | async-done | bytes 4194320 | tf_op jit(solution)/shard_map/all_gather | solution.py:40
  307.1 1.0 constant_dynamic-slice_fusion
  308.0 0.0 copy-done.1
  308.0 0.0 copy-start
  308.0 0.3 fusion.5
  308.4 32.8 %psum.7 = f32[16]{0:T(128)S(1)} all-reduce(f32[16]{0:T(128)S(1)} %fusion.5), channel_id=1, replica_groups=mesh['fsdp'=32,'tp'=16] {'tp'}, use_global_device_ids=true, to_apply=%region_2.3 | all-reduce | flops 16 | bytes 128 | tf_op jit(solution)/shard_map/psum | solution.py:49
  341.1 0.5 multiply_bitcast_fusion
  341.7 0.0 copy-done
  (3 shorter events, 0.0 us)
Async XLA Ops:
  7.2 81.1 %all-gather.4.cloned.1.call-start = ((), (), s32[]{:S(2)}) async-start(), calls=%async_computation | async-start | bytes 4456448 | tf_op jit(solution)/shard_map/all_gather | solution.py:27
  10.1 201.9 %all-gather.6.cloned.1.call-start = ((), (), s32[]{:S(2)}) async-start(), calls=%async_computation.1 | async-start | bytes 6488064 | tf_op jit(solution)/shard_map/all_gather | solution.py:32
  10.9 296.2 %all-gather.8.cloned.1.call-start = ((), (), s32[]{:S(2)}) async-start(), calls=%async_computation.2 | async-start | bytes 4456448 | tf_op jit(solution)/shard_map/all_gather | solution.py:40
  12.8 207.8 %copy-start.2 = (s32[1,16]{1,0:T(1,128)S(1)}, s32[1,16]{1,0:T(1,128)}, u32[]{:S(2)}) copy-start(s32[1,16]{1,0:T(1,128)} %param.12) | copy-start | bytes 196
  12.8 295.2 %copy-start.1 = (f32[4096]{0:T(1024)S(1)}, f32[4096]{0:T(1024)}, u32[]{:S(2)}) copy-start(f32[4096]{0:T(1024)} %param.13) | copy-start | bytes 49156
  308.0 33.6 %copy-start = (bf16[32,4096]{1,0:T(8,128)(2,1)}, bf16[32,4096]{1,0:T(8,128)(2,1)S(1)}, u32[]{:S(2)}) copy-start(bf16[32,4096]{1,0:T(8,128)(2,1)S(1)} %constant_dynamic-slice_fusion) | copy-start | bytes 786436
Sparse Core Ops, SparseCore 0:
  11.9 76.3 all-gather.3
  90.4 121.6 all-gather.5
  220.8 86.2 all-gather.7
where the time goes:
time: 348 us
  waiting for transfers between devices  286 us (82%)
  blocking collectives  32.8 us (9%)
  between operations  13.8 us (4%)
  matrix products  7.37 us (2%)
  other arithmetic  5.98 us (2%)
    all_gather x1, waiting for transfers between devices, local(): lax.all_gather(proj_weight, 'fsdp', axis=1, tiled=True)  124 us
    all_gather x1, waiting for transfers between devices, local(): full_rows = lax.all_gather(mixed_local, 'tp', axis=1, tiled=True)  86.4 us
    all_gather x1, waiting for transfers between devices, local(): slab_rows = lax.all_gather(normed, 'tp', axis=0, tiled=True)  75.4 us
    psum x1, blocking collectives, local(): summed_score = lax.psum(partial_sum, 'tp')  32.8 us
    dot_general x1, matrix products, local(): jnp.einsum('sk,ikc->isc', slab_rows, lax.all_gather(proj_weight, 'fsdp',...  7.03 us
  transfers between devices with their start and end apart: 3, of which 3 were waited for; matrix products, arithmetic and copies ran while one was open for 1% of the time, Pallas kernels for 0%

commit v1 on v0

--- a/solution.py
+++ b/solution.py
@@ -1,3 +1,4 @@
+import functools
 import math
 import jax
 import jax.numpy as jnp
@@ -5,6 +6,15 @@
 from jax.sharding import PartitionSpec as P
 
 EPSILON = 1e-06
+
+
+def measure_lane_all(my_tile, peer_axis):
+    return jnp.concatenate(
+        jax.lax.all_to_all(jnp.stack([my_tile] * jax.lax.psum(1, peer_axis)), peer_axis, 0, 0), 1
+    )
+
+
+end_the_samples_all = functools.partial(measure_lane_all, peer_axis="fsdp")
 
 
 def short_conv(gated_prod, tap_table, segments):
@@ -29,7 +39,7 @@
     projected = jnp.einsum(
         "sk,ikc->isc",
         slab_rows,
-        lax.all_gather(proj_weight, "fsdp", axis=1, tiled=True),
+        end_the_samples_all(proj_weight),
         preferred_element_type=jnp.float32,
     )
     gated_prod = projected[1] * projected[2]

time: 348 us -> 431 us (1.24)
  waiting for transfers between devices: 286 us -> 345 us
  starting transfers between devices: 0.12 us -> 17.3 us
  local copies, waits for them, and re-layouts: 1.84 us -> 11.7 us
    all_to_all x0 -> x1, waiting for transfers between devices: none -> 272 us  [measure_lane_all(): jax.lax.all_to_all(jnp.stack([my_tile] * jax.lax.psum(1, peer_axis)), pee...]
    all_gather x1 -> x0, waiting for transfers between devices: 124 us -> none  [local(): lax.all_gather(proj_weight, 'fsdp', axis=1, tiled=True)]
    all_gather x1, waiting for transfers between devices: 75.4 us -> 0.01 us  [local(): slab_rows = lax.all_gather(normed, 'tp', axis=0, tiled=True)]
    all_to_all x0 -> x1, starting transfers between devices: none -> 17.2 us  [measure_lane_all(): jax.lax.all_to_all(jnp.stack([my_tile] * jax.lax.psum(1, peer_axis)), pee...]
    all_gather x1, waiting for transfers between devices: 86.4 us -> 72.5 us  [local(): full_rows = lax.all_gather(mixed_local, 'tp', axis=1, tiled=True)]
    reshape x0 -> x1, local copies, waits for them, and re-layouts: none -> 6.21 us  [measure_lane_all(): jnp.concatenate(jax.lax.all_to_all(jnp.stack([my_tile] * jax.lax.psum(1,...]
    another operation x0 -> x1, local copies, waits for them, and re-layouts: none -> 4.33 us  [measure_lane_all(): jnp.stack([my_tile] * jax.lax.psum(1, peer_axis))]
  transfers between devices with their start and end apart: 3 -> 3, of which waited for: 3 -> 2; matrix products, arithmetic and copies ran while one was open for 1% -> 2% of each run, Pallas kernels for 0% -> 0%
where the time goes in v1:
time: 431 us
  waiting for transfers between devices  345 us (80%)
  blocking collectives  32.8 us (8%)
  starting transfers between devices  17.3 us (4%)
  between operations  14.2 us (3%)
  local copies, waits for them, and re-layouts  11.7 us (3%)
  matrix products  7.39 us (2%)
    all_to_all x1, waiting for transfers between devices, measure_lane_all(): jax.lax.all_to_all(jnp.stack([my_tile] * jax.lax.psum(1, peer_axis)), pee...  272 us
    all_gather x1, waiting for transfers between devices, local(): full_rows = lax.all_gather(mixed_local, 'tp', axis=1, tiled=True)  72.5 us
    psum x1, blocking collectives, local(): summed_score = lax.psum(partial_sum, 'tp')  32.8 us
    all_to_all x1, starting transfers between devices, measure_lane_all(): jax.lax.all_to_all(jnp.stack([my_tile] * jax.lax.psum(1, peer_axis)), pee...  17.2 us
  transfers between devices with their start and end apart: 3, of which 2 were waited for; matrix products, arithmetic and copies ran while one was open for 2% of the time, Pallas kernels for 0%

profile of v1, /device:TPU:1, one launch (start us, length us, event | category | flops | bytes accessed | tf_op | source)
XLA Modules:
  0.0 431.2 jit_solution(14965672320211528066)
XLA Ops:
  7.2 4.3 %stack.2 = bf16[32,3,128,256]{3,2,1,0:T(8,128)(2,1)} broadcast(bf16[3,128,256]{2,1,0:T(8,128)(2,1)} %param.9), dimensions={1,2,3} | broadcast | bytes 6488064 | tf_op jit(solution)/shard_map/stack | solution.py:13
  11.5 0.0 copy-start
  11.5 0.0 copy-start.2
  11.5 0.0 copy-start.3
  11.5 0.0 copy-start.4
  11.5 17.2 %all-to-all-start = ((bf16[32,3,128,256]{3,2,1,0:T(8,128)(2,1)}), bf16[32,3,128,256]{3,2,1,0:T(8,128)(2,1)}, u32[]{:S(2)}, u32[]{:S(2)}) async-start(bf16[32,3,128,256]{3,2,1,0:T(8,128)(2,1)} %stack.2), calls=%async_computation | async-start | bytes 12582912 | tf_op jit(solution)/shard_map/all_to_all | solution.py:13
  28.7 0.0 all-gather.3.cloned.1.call-start
  28.8 0.0 copy-done
  28.8 0.2 fusion.26
  29.0 0.0 copy-done.2
  29.0 0.8 fusion.28
  29.8 0.0 all-gather.3.cloned.1.call-update
  29.8 0.0 all-gather.5.cloned.1.call-start
  29.9 0.0 copy-done.3
  29.9 0.1 broadcast_in_dim.4
  30.0 0.1 reshape.48
  30.1 0.0 copy-done.4
  30.1 0.1 fusion.42
  30.2 272.3 %all-to-all-done = bf16[32,3,128,256]{3,2,1,0:T(8,128)(2,1)} async-done(((bf16[32,3,128,256]{3,2,1,0:T(8,128)(2,1)}), bf16[32,3,128,256]{3,2,1,0:T(8,128)(2,1)}, u32[]{:S(2)}, u32[]{:S(2)}) %all-to-all-start) | async-done | bytes 6291488 | tf_op jit(solution)/shard_map/all_to_all | solution.py:13
  302.4 6.2 %copy.10 = bf16[3,32,128,256]{3,2,1,0:T(8,128)(2,1)} copy(bf16[3,32,128,256]{3,2,0,1:T(8,128)(2,1)} %bitcast.1) | data formatting | bytes 12582912 | tf_op jit(solution)/shard_map/reshape | solution.py:12
  308.6 0.0 all-gather.3.cloned.1.call-done
  308.6 0.0 copy-start.6
  308.6 0.0 copy-start.5
  308.6 7.1 %fusion.2 = f32[3,512,256]{2,1,0:T(8,128)S(1)} fusion(bf16[3,4096,256]{2,1,0:T(8,128)(2,1)} %bitcast.31, bf16[512,4096]{1,0:T(8,128)(2,1)} %all-gather.3.cloned.1.call-done), kind=kOutput, calls=%fused_computation.3 | convolution fusion | flops 3221225472 | bytes 12058624 | tf_op jit(solution)/shard_map/sk,ikc->isc/dot_general | solution.py:39
  315.7 0.1 fusion.29
  315.8 1.5 fusion.15
  317.2 0.0 all-gather.5.cloned.1.call-update
  317.3 0.0 copy-done.6
  317.3 72.5 %all-gather.5.cloned.1.call-done = bf16[512,4096]{1,0:T(8,128)(2,1)} async-done(((bf16[512,256]{1,0:T(8,128)(2,1)}), bf16[512,4096]{1,0:T(8,128)(2,1)}) %all-gather.5.cloned.1.call-update) | async-done | bytes 4194320 | tf_op jit(solution)/shard_map/all_gather | solution.py:50
  389.7 1.0 constant_dynamic-slice_fusion
  390.7 0.0 copy-done.5
  390.7 0.0 copy-start.1
  390.7 0.3 fusion.5
  391.1 32.8 %psum.7 = f32[16]{0:T(128)S(1)} all-reduce(f32[16]{0:T(128)S(1)} %fusion.5), channel_id=1, replica_groups=mesh['fsdp'=32,'tp'=16] {'tp'}, use_global_device_ids=true, to_apply=%region_2.3 | all-reduce | flops 16 | bytes 128 | tf_op jit(solution)/shard_map/psum | solution.py:59
  423.8 0.5 multiply_bitcast_fusion
  424.4 0.0 copy-done.1
  (3 shorter events, 0.0 us)
Async XLA Ops:
  11.5 17.3 %copy-start = (bf16[32,4096]{1,0:T(8,128)(2,1)S(1)}, bf16[32,4096]{1,0:T(8,128)(2,1)}, u32[]{:S(2)}) copy-start(bf16[32,4096]{1,0:T(8,128)(2,1)} %param.7) | copy-start | bytes 786436
  11.5 17.5 %copy-start.2 = (f32[4096]{0:T(1024)S(1)}, f32[4096]{0:T(1024)}, u32[]{:S(2)}) copy-start(f32[4096]{0:T(1024)} %param.8) | copy-start | bytes 49156
  11.5 18.4 %copy-start.3 = (f32[16,7]{0,1:T(8,128)S(1)}, f32[16,7]{0,1:T(8,128)}, u32[]{:S(2)}) copy-start(f32[16,7]{0,1:T(8,128)} %param.10) | copy-start | bytes 1348
  11.5 18.6 %copy-start.4 = (s32[1,512]{1,0:T(1,128)S(1)}, s32[1,512]{1,0:T(1,128)}, u32[]{:S(2)}) copy-start(s32[1,512]{1,0:T(1,128)} %param.11) | copy-start | bytes 6148
  11.5 290.9 %all-to-all-start = ((bf16[32,3,128,256]{3,2,1,0:T(8,128)(2,1)}), bf16[32,3,128,256]{3,2,1,0:T(8,128)(2,1)}, u32[]{:S(2)}, u32[]{:S(2)}) async-start(bf16[32,3,128,256]{3,2,1,0:T(8,128)(2,1)} %stack.2), calls=%async_computation | async-start | bytes 12582912 | tf_op jit(solution)/shard_map/all_to_all | solution.py:13
  28.7 279.9 %all-gather.3.cloned.1.call-start = ((), (), s32[]{:S(2)}) async-start(), calls=%async_computation.1 | async-start | bytes 4456448 | tf_op jit(solution)/shard_map/all_gather | solution.py:37
  29.8 359.9 %all-gather.5.cloned.1.call-start = ((), (), s32[]{:S(2)}) async-start(), calls=%async_computation.2 | async-start | bytes 4456448 | tf_op jit(solution)/shard_map/all_gather | solution.py:50
  308.6 8.6 %copy-start.6 = (s32[1,16]{1,0:T(1,128)S(1)}, s32[1,16]{1,0:T(1,128)}, u32[]{:S(2)}) copy-start(s32[1,16]{1,0:T(1,128)} %param.12) | copy-start | bytes 196
  308.6 82.1 %copy-start.5 = (f32[4096]{0:T(1024)S(1)}, f32[4096]{0:T(1024)}, u32[]{:S(2)}) copy-start(f32[4096]{0:T(1024)} %param.13) | copy-start | bytes 49156
  390.7 33.6 %copy-start.1 = (bf16[32,4096]{1,0:T(8,128)(2,1)}, bf16[32,4096]{1,0:T(8,128)(2,1)S(1)}, u32[]{:S(2)}) copy-start(bf16[32,4096]{1,0:T(8,128)(2,1)S(1)} %constant_dynamic-slice_fusion) | copy-start | bytes 786436
Sparse Core Ops, SparseCore 0:
  33.5 76.8 all-gather.2
  317.4 72.3 all-gather.4
